TPU v7x, 32 devices: a whole 2x2x4 slice. The times are simulated.
32 devices in a mesh: groups: 2 (over x), wide: 4 (over y, core), expert: 4 (over z).
Axes of the slice: x: 2, y: 2, z: 4, core: 2. Of those that a mesh axis runs over, the one named last changes fastest.
Arguments:
- prompts: bfloat16 [8, 128, 6144], P(('groups', 'wide'), None, 'expert'), parts along dimension 0, may hold values from -6 to 6
- span_slot_owner: int32 [8], P('groups'), parts along dimension 0, may hold values from 0 to 3, as said below
- row_expert_index: int32 [768, 2], P('groups'), parts along dimension 0, may hold values from 0 to 7, all different within a row
- tile_tenant_index: int32 [6], P('groups'), parts along dimension 0, may hold values from 0 to 7
- tenant_adapter_slot: int32 [16], P('groups'), parts along dimension 0, may hold values from 0 to 7, each once
- router: bfloat16 [6144, 8], replicated, may hold values from -0.078125 to 0.078125
- gate_weight: bfloat16 [2, 6144, 16384], P(None, None, ('wide', 'expert')), may hold values from -0.078125 to 0.078125
- up_weight: bfloat16 [2, 6144, 16384], P(None, None, ('wide', 'expert')), may hold values from -0.078125 to 0.078125
- down_weight: bfloat16 [2, 16384, 6144], P(None, 'wide', 'expert'), may hold values from -0.046875 to 0.046875
- adapter_down_weight: bfloat16 [16, 2, 6144, 64], P(('groups', 'wide'), None, 'expert'), parts along dimension 0, may hold values from -0.078125 to 0.078125
- adapter_up_weight: bfloat16 [16, 2, 64, 16384], P('groups', None, None, ('wide', 'expert')), parts along dimension 0, may hold values from -0.75 to 0.75
Outputs:
- mixed: bfloat16 [768, 6144], P(('groups', 'wide'), 'expert'), parts along dimension 0
There are 2 independent parts, one for each index of `groups`. A program takes and returns all parts, laid end to end along the dimension named above; an argument that names none is the same for every part. Nothing has to cross between parts.
Inputs may be any that keep to these rules, and one draw needn't show every extreme that they name: `span_slot_owner`: a permutation of the slots; span c, for c < 3, is in slot span_slot_owner[c]. `row_expert_index`: each row names two different experts. `tenant_adapter_slot`: a permutation of the slots. `tile_tenant_index`: tenant of rows 128 * i to 128 * i + 127.
All inputs are finite; a program needn't handle non-finite values.
Results may differ from a plain program's by a relative error of at most 0.0051.
Values may be sent and summed in bfloat16 or wider, within the bound.
No kernel may reach another device: no remote copies, remote signals or barrier semaphores. Data moves between devices by JAX's collectives and lax.ppermute only.
A program may use at most 128 MiB of HBM per device.

v0:
```python
import jax
import jax.numpy as jnp
from jax import lax
from jax.sharding import PartitionSpec as P

NCHUNK = 3
ADAPTER_SCALE = 0.5


def spread(block, axis, source):
    block = jnp.where(lax.axis_index(axis) == source, block, jnp.zeros_like(block))
    return lax.psum(block, axis)


def per_device(
    prompts,
    span_slot_owner,
    row_expert_index,
    tile_tenant_index,
    tenant_adapter_slot,
    router,
    gate_weight,
    up_weight,
    down_weight,
    adapter_down_weight,
    adapter_up_weight,
):
    column = lax.axis_index("expert")
    own_slot = prompts[0]
    width_part = own_slot.shape[1]
    full_slot = lax.all_gather(own_slot, "expert", axis=1, tiled=True)
    pieces = [
        spread(full_slot, "wide", span_slot_owner[span_index]) for span_index in range(NCHUNK)
    ]
    input_rows = jnp.concatenate(pieces, axis=0)
    slices = lax.dynamic_slice_in_dim(input_rows, column * width_part, width_part, 1)
    tokens = input_rows.shape[0]
    window = gate_weight.shape[0]
    logits = jnp.dot(input_rows, router, preferred_element_type=jnp.float32)
    experts = jnp.arange(router.shape[1], dtype=jnp.int32)
    picked = (row_expert_index[:, :, None] == experts[None, None, :]).astype(jnp.float32)
    chosen = jnp.sum(picked * logits[:, None, :], axis=2)
    first_prob = jax.nn.sigmoid(chosen[:, 0] - chosen[:, 1])
    second_prob = jax.nn.sigmoid(chosen[:, 1] - chosen[:, 0])
    weight = (
        first_prob[:, None] * picked[:, 0, :window] + second_prob[:, None] * picked[:, 1, :window]
    )
    tile_count = tile_tenant_index.shape[0]
    tile_rows = tokens // tile_count
    resident_slots = adapter_down_weight.shape[0]
    tile_slot_index = jnp.take(tenant_adapter_slot, tile_tenant_index)
    owners = tile_slot_index // resident_slots
    local_expert_index = tile_slot_index % resident_slots
    tile_slices = slices.reshape(tile_count, tile_rows, width_part)

    def fetch_one(state_carry, tile_position):
        adapter_piece = lax.dynamic_index_in_dim(
            adapter_down_weight, local_expert_index[tile_position], 0, keepdims=False
        )
        return (state_carry, spread(adapter_piece, "wide", owners[tile_position]))

    unused, fetched = lax.scan(fetch_one, jnp.int32(0), jnp.arange(tile_count, dtype=jnp.int32))
    partial_rank = jnp.einsum(
        "ntd,nedr->nter", tile_slices, fetched, preferred_element_type=jnp.float32
    )
    summed = lax.psum(partial_rank, "expert")
    lowrank = summed.astype(jnp.bfloat16)
    tenant_list = adapter_up_weight.shape[0]
    select_tenant = (
        tile_tenant_index[:, None] == jnp.arange(tenant_list, dtype=jnp.int32)[None, :]
    ).astype(adapter_up_weight.dtype)
    tile_up = jnp.einsum(
        "cj,jvqz->cvqz", select_tenant, adapter_up_weight, preferred_element_type=jnp.float32
    ).astype(jnp.bfloat16)
    adapted_hidden = jnp.einsum(
        "nter,nerf->ntef", lowrank, tile_up, preferred_element_type=jnp.float32
    )
    adapted_hidden = adapted_hidden.reshape(tokens, window, adapted_hidden.shape[3])
    gate_pre = jnp.einsum(
        "td,edf->tef", input_rows, gate_weight, preferred_element_type=jnp.float32
    )
    up_projection_value = (
        jnp.einsum("td,edf->tef", input_rows, up_weight, preferred_element_type=jnp.float32)
        + ADAPTER_SCALE * adapted_hidden
    )
    hidden = (weight[:, :, None] * jax.nn.silu(gate_pre) * up_projection_value).astype(jnp.bfloat16)
    partial_out = jnp.einsum(
        "tef,efd->td",
        lax.all_gather(hidden, "expert", axis=2, tiled=True),
        down_weight,
        preferred_element_type=jnp.float32,
    )
    mixed_rows = lax.psum_scatter(partial_out, "wide", scatter_dimension=0, tiled=True)
    return mixed_rows.astype(jnp.bfloat16)


def solution(mesh):
    in_specs = (
        P(("groups", "wide"), None, "expert"),
        P("groups"),
        P("groups", None),
        P("groups"),
        P("groups"),
        P(),
        P(None, None, ("wide", "expert")),
        P(None, None, ("wide", "expert")),
        P(None, "wide", "expert"),
        P(("groups", "wide"), None, "expert", None),
        P("groups", None, None, ("wide", "expert")),
    )
    out_specs = P(("groups", "wide"), "expert")
    return jax.shard_map(
        per_device, mesh=mesh, in_specs=in_specs, out_specs=out_specs, check_vma=False
    )
```

profile of v0, /device:TPU:0, one launch (start us, length us, event | category | flops | bytes accessed | tf_op | source)
XLA Modules:
  0.0 514.7 jit_solution(17569741497082177469)
XLA Ops:
  7.3 1.4 fusion.18
  10.5 38.3 %all-gather.6.cloned.1.call-done = bf16[1,128,6144]{2,1,0:T(8,128)(2,1)} async-done(((bf16[1,128,1536]{2,1,0:T(8,128)(2,1)}), bf16[1,128,6144]{2,1,0:T(8,128)(2,1)}) %all-gather.6.cloned.1.call-update) | async-done | bytes 1572880 | tf_op jit(solution)/shard_map/all_gather | solution.py:31
  48.8 3.7 select_bitcast_fusion
  53.8 2.5 fusion.6
  56.3 89.6 %all-reduce.5.cloned.1.call-done = (bf16[128,6144]{1,0:T(8,128)(2,1)}, bf16[128,6144]{1,0:T(8,128)(2,1)}, bf16[128,6144]{1,0:T(8,128)(2,1)}) async-done(((bf16[128,6144]{1,0:T(8,128)(2,1)}, bf16[128,6144]{1,0:T(8,128)(2,1)}, bf16[128,6144]{1,0:T(8,128)(2,1)}), (bf16[128,6144]{1,0:T(8,128)(2,1)}, bf16[128,6144]{1,0:T(8,128)(2,1)}, bf16[128,6144]{1,0:T(8,128)(2,1)})) %all-reduce.5.cloned.1.call-update) | async-done | bytes 4718608 | tf_op jit(solution)/shard_map/psum | solution.py:12
  145.9 1.7 constant_dynamic-update-slice_fusion.3
  148.8 1.3 fusion.19
  150.9 134.1 %while.10 = (s32[]{:T(128)}, bf16[3,2,1536,64]{3,2,1,0:T(8,128)(2,1)}, s32[3]{0:T(128)S(1)}, s32[3]{0:T(128)S(1)}, s32[3]{0:T(128)S(1)}, /*index=5*/bf16[2,2,153...) while((s32[]{:T(128)}, ...), condition=%wide.region_6.7_spmd, body=%wide.region_4.6_spmd.sunk | while | flops 393228 | bytes 7078207 | solution.py:62
  157.6 1.0 broadcast_select_fusion.2
  158.7 34.9 %all-reduce.7.cloned.1.call-done = bf16[1,2,1536,64]{3,2,1,0:T(8,128)(2,1)} async-done(((bf16[1,2,1536,64]{3,2,1,0:T(8,128)(2,1)}), bf16[1,2,1536,64]{3,2,1,0:T(8,128)(2,1)}) %all-reduce.7.cloned.1.call-update) | async-done | bytes 393232 | tf_op jit(solution)/shard_map/while/body/eval_jaxpr/psum | solution.py:12
  193.6 2.1 constant_dynamic-update-slice_fusion.5
  203.4 34.8 %all-reduce.7.cloned.1.call-done = bf16[1,2,1536,64]{3,2,1,0:T(8,128)(2,1)} async-done(((bf16[1,2,1536,64]{3,2,1,0:T(8,128)(2,1)}), bf16[1,2,1536,64]{3,2,1,0:T(8,128)(2,1)}) %all-reduce.7.cloned.1.call-update) | async-done | bytes 393232 | tf_op jit(solution)/shard_map/while/body/eval_jaxpr/psum | solution.py:12
  238.2 2.1 constant_dynamic-update-slice_fusion.5
  248.1 34.8 %all-reduce.7.cloned.1.call-done = bf16[1,2,1536,64]{3,2,1,0:T(8,128)(2,1)} async-done(((bf16[1,2,1536,64]{3,2,1,0:T(8,128)(2,1)}), bf16[1,2,1536,64]{3,2,1,0:T(8,128)(2,1)}) %all-reduce.7.cloned.1.call-update) | async-done | bytes 393232 | tf_op jit(solution)/shard_map/while/body/eval_jaxpr/psum | solution.py:12
  282.9 2.1 constant_dynamic-update-slice_fusion.5
  285.0 2.6 fusion.20
  287.6 22.5 %all-reduce.8 = bf16[3,128,2,64]{1,3,2,0:T(8,128)(2,1)S(1)} all-reduce(f32[3,128,2,64]{1,3,2,0:T(8,128)S(1)} %fusion.20), channel_id=1, replica_groups=mesh['groups'=2,'wide'=4,'expert'=4] {'expert'}, use_global_device_ids=true, to_apply=%region_7.8 | all-reduce | flops 49152 | bytes 294912 | tf_op jit(solution)/shard_map/psum | solution.py:66
  311.1 1.2 slice-done.1
  312.2 15.1 %fusion.2 = f32[384,2,1024]{2,0,1:T(8,128)} fusion(bf16[2,6144,1024]{2,1,0:T(8,128)(2,1)} %param.19, bf16[384,6144]{1,0:T(8,128)(2,1)S(1)} %bitcast.68), kind=kOutput, calls=%fused_computation.6 | convolution fusion | flops 9663676416 | bytes 33030144 | tf_op jit(solution)/shard_map/td,edf->tef/dot_general | solution.py:79
  327.4 16.2 %fusion.5 = bf16[384,2,1024]{2,0,1:T(8,128)(2,1)} fusion(f32[3,128,2,1024]{3,1,0,2:T(8,128)S(1)} %copy.15, f32[384,2,1024]{2,0,1:T(8,128)} %fusion.2, f32[384,2]{0,1:T(2,128)S(1)} %fusion.13, bf16[2,6144,1024]{2,1,0:T(8,128)(2,1)} %param.20, bf16[384,6144]{1,0:T(8,128)(2,1)S(1)} %bitcast.68), kind=kOutput, calls=%fused_computation.10 | convolution fusion | flops 9669967872 | bytes 37751808 | tf_op jit(solution)/shard_map/td,edf->tef/dot_general | solution.py:83
  343.7 113.3 %all-gather.4.cloned.1.call-done = bf16[384,2,4096]{2,0,1:T(8,128)(2,1)} async-done(((bf16[384,2,1024]{2,0,1:T(8,128)(2,1)}), bf16[384,2,4096]{2,0,1:T(8,128)(2,1)}) %all-gather.4.cloned.1.call-update) | async-done | bytes 6291472 | tf_op jit(solution)/shard_map/all_gather | solution.py:89
  456.9 17.7 %convolution_bitcast_fusion = f32[384,1536]{1,0:T(8,128)} fusion(bf16[384,2,4096]{2,0,1:T(8,128)(2,1)} %all-gather.4.cloned.1.call-done, bf16[2,4096,1536]{2,1,0:T(8,128)(2,1)} %param.21), kind=kOutput, calls=%fused_computation.12 | convolution fusion | flops 9663676416 | bytes 33816576 | tf_op jit(solution)/shard_map/tef,efd->td/dot_general | solution.py:87
  474.6 31.4 %reduce-scatter.2.cloned.1.call-done = f32[96,1536]{1,0:T(8,128)} async-done(((f32[384,1536]{1,0:T(8,128)}), f32[96,1536]{1,0:T(8,128)}) %reduce-scatter.2.cloned.1.call-update) | async-done | bytes 589840 | tf_op jit(solution)/shard_map/reduce_scatter | solution.py:93
  506.0 1.8 convert_element_type.20
  (73 shorter events, 13.7 us)
Async XLA Ops:
  6.5 47.3 %copy-start = (bf16[8,2,64,1024]{3,2,1,0:T(8,128)(2,1)S(1)}, bf16[8,2,64,1024]{3,2,1,0:T(8,128)(2,1)}, u32[]{:S(2)}) copy-start(bf16[8,2,64,1024]{3,2,1,0:T(8,128)(2,1)} %param.23) | copy-start | bytes 6291460
  6.5 42.2 %all-gather.6.cloned.1.call-start = ((), (), s32[]{:S(2)}) async-start(), calls=%async_computation.3 | async-start | bytes 1966080 | tf_op jit(solution)/shard_map/all_gather | solution.py:31
  7.3 138.6 %all-reduce.5.cloned.1.call-start = ((), (), s32[]{:S(2)}) async-start(), calls=%async_computation.4 | async-start | bytes 9437184 | tf_op jit(solution)/shard_map/psum | solution.py:12
  52.4 0.7 copy-start.10
  52.4 0.7 copy-start.2
  52.4 1.3 copy-start.9
  145.9 1.9 copy-start.7
  145.9 2.4 copy-start.6
  147.8 1.0 copy-start.8
  148.8 2.1 copy-start.3
  148.8 2.1 copy-start.4
  150.9 42.7 %all-reduce.7.cloned.1.call-start = ((), (), s32[]{:S(2)}) async-start(), calls=%async_computation.5 | async-start | bytes 1572864 | tf_op jit(solution)/shard_map/while/body/eval_jaxpr/psum | solution.py:12
  195.7 42.6 %all-reduce.7.cloned.1.call-start = ((), (), s32[]{:S(2)}) async-start(), calls=%async_computation.5 | async-start | bytes 1572864 | tf_op jit(solution)/shard_map/while/body/eval_jaxpr/psum | solution.py:12
  240.3 42.6 %all-reduce.7.cloned.1.call-start = ((), (), s32[]{:S(2)}) async-start(), calls=%async_computation.5 | async-start | bytes 1572864 | tf_op jit(solution)/shard_map/while/body/eval_jaxpr/psum | solution.py:12
  285.0 25.1 %copy-start.5 = (bf16[3,2,64,1024]{3,0,2,1:T(4,128)(2,1)S(1)}, bf16[3,2,64,1024]{3,0,2,1:T(4,128)(2,1)}, u32[]{:S(2)}) copy-start(bf16[3,2,64,1024]{3,0,2,1:T(4,128)(2,1)} %fusion.6) | copy-start | bytes 2359300
  285.0 171.9 %all-gather.4.cloned.1.call-start = ((), (), s32[]{:S(2)}) async-start(), calls=%async_computation.1 | async-start | bytes 7864320 | tf_op jit(solution)/shard_map/all_gather | solution.py:89
  285.0 26.1 %slice-start = ((s8[4718592]{0:T(1024)(128)(4,1)}), s8[524288]{0:T(1024)(128)(4,1)S(1)}, s32[]{:S(2)}) async-start(s8[4718592]{0:T(1024)(128)(4,1)} %bitcast.67), calls=%async_computation.6 | async-start | bytes 1048576
  310.1 2.2 slice-start.1
  343.6 162.4 %reduce-scatter.2.cloned.1.call-start = ((), (), s32[]{:S(2)}) async-start(), calls=%async_computation.2 | async-start | bytes 2949120 | tf_op jit(solution)/shard_map/reduce_scatter | solution.py:93
  456.9 50.9 %copy-start.1 = (bf16[8,2,64,1024]{3,2,1,0:T(8,128)(2,1)S(1)}, bf16[8,2,64,1024]{3,2,1,0:T(8,128)(2,1)}, u32[]{:S(2)}) copy-start(bf16[8,2,64,1024]{3,2,1,0:T(8,128)(2,1)} %param.23) | copy-start | bytes 6291460
Sparse Core Ops, SparseCore 0:
  8.9 39.7 all-gather.5
  52.6 93.2 all-reduce.4
  158.8 34.7 all-reduce.6
  203.5 34.6 all-reduce.6
  248.2 34.6 all-reduce.6
  343.7 113.1 all-gather.3
  474.7 31.2 reduce-scatter.1
where the time goes:
time: 515 us
  waiting for transfers between devices  378 us (73%)
  matrix products  56.1 us (11%)
  blocking collectives  22.5 us (4%)
  local copies, waits for them, and re-layouts  20.4 us (4%)
  between operations  15.4 us (3%)
  loops' own time  13.7 us (3%)
  other arithmetic  8.61 us (2%)
    psum x4, waiting for transfers between devices, spread(): return lax.psum(block, axis)  194 us
    all_gather x1, waiting for transfers between devices, per_device(): lax.all_gather(hidden, 'expert', axis=2, tiled=True)  113 us
    all_gather x1, waiting for transfers between devices, per_device(): full_slot = lax.all_gather(own_slot, 'expert', axis=1, tiled=True)  38.3 us
    reduce_scatter x1, waiting for transfers between devices, per_device(): lax.psum_scatter(partial_out, 'wide', scatter_dimension=0, tiled=True)  31.4 us
    psum x1, blocking collectives, per_device(): summed = lax.psum(partial_rank, 'expert')  22.5 us
    dot_general x1, matrix products, per_device(): jnp.einsum('tef,efd->td', lax.all_gather(hidden, 'expert', axis=2, tiled=...  17.7 us
    dot_general x1, matrix products, per_device(): jnp.einsum('td,edf->tef', input_rows, up_weight, preferred_element_type=j...  16.2 us
    dot_general x1, matrix products, per_device(): jnp.einsum('td,edf->tef', input_rows, gate_weight, preferred_element_type...  15.1 us
  transfers between devices with their start and end apart: 7, of which 7 were waited for; matrix products, arithmetic and copies ran while one was open for 1% of the time, Pallas kernels for 0%

commit v1 on v0

--- a/solution.py
+++ b/solution.py
@@ -63,7 +63,7 @@
     partial_rank = jnp.einsum(
         "ntd,nedr->nter", tile_slices, fetched, preferred_element_type=jnp.float32
     )
-    summed = lax.psum(partial_rank, "expert")
+    summed = jnp.sum(lax.all_gather(partial_rank, "expert"), axis=0)
     lowrank = summed.astype(jnp.bfloat16)
     tenant_list = adapter_up_weight.shape[0]
     select_tenant = (

time: 515 us -> 513 us (level)
    psum x1 -> x0, blocking collectives: 22.5 us -> none  [per_device(): summed = lax.psum(partial_rank, 'expert')]
    all_gather x0 -> x1, blocking collectives: none -> 19.7 us  [per_device(): summed = jnp.sum(lax.all_gather(partial_rank, 'expert'), axis=0)]
where the time goes in v1:
time: 513 us
  waiting for transfers between devices  378 us (74%)
  matrix products  55.7 us (11%)
  local copies, waits for them, and re-layouts  21 us (4%)
  blocking collectives  19.7 us (4%)
  between operations  15.4 us (3%)
  loops' own time  13.7 us (3%)
  other arithmetic  8.44 us (2%)
    psum x4, waiting for transfers between devices, spread(): return lax.psum(block, axis)  194 us
    all_gather x1, waiting for transfers between devices, per_device(): lax.all_gather(hidden, 'expert', axis=2, tiled=True)  114 us
    all_gather x1, waiting for transfers between devices, per_device(): full_slot = lax.all_gather(own_slot, 'expert', axis=1, tiled=True)  38.3 us
    reduce_scatter x1, waiting for transfers between devices, per_device(): lax.psum_scatter(partial_out, 'wide', scatter_dimension=0, tiled=True)  31.4 us
    all_gather x1, blocking collectives, per_device(): summed = jnp.sum(lax.all_gather(partial_rank, 'expert'), axis=0)  19.7 us
    dot_general x1, matrix products, per_device(): jnp.einsum('tef,efd->td', lax.all_gather(hidden, 'expert', axis=2, tiled=...  17.7 us
    dot_general x1, matrix products, per_device(): jnp.einsum('td,edf->tef', input_rows, up_weight, preferred_element_type=j...  16.2 us
    dot_general x1, matrix products, per_device(): jnp.einsum('td,edf->tef', input_rows, gate_weight, preferred_element_type...  15.1 us
  transfers between devices with their start and end apart: 7, of which 7 were waited for; matrix products, arithmetic and copies ran while one was open for 1% of the time, Pallas kernels for 0%

profile of v1, /device:TPU:0, one launch (start us, length us, event | category | flops | bytes accessed | tf_op | source)
XLA Modules:
  0.0 512.6 jit_solution(12138929332741206548)
XLA Ops:
  7.3 1.4 fusion.22
  10.5 38.3 %all-gather.7.cloned.1.call-done = bf16[1,128,6144]{2,1,0:T(8,128)(2,1)} async-done(((bf16[1,128,1536]{2,1,0:T(8,128)(2,1)}), bf16[1,128,6144]{2,1,0:T(8,128)(2,1)}) %all-gather.7.cloned.1.call-update) | async-done | bytes 1572880 | tf_op jit(solution)/shard_map/all_gather | solution.py:31
  48.8 3.7 select_bitcast_fusion
  53.8 2.4 fusion.10
  56.2 89.6 %all-reduce.4.cloned.1.call-done = (bf16[128,6144]{1,0:T(8,128)(2,1)}, bf16[128,6144]{1,0:T(8,128)(2,1)}, bf16[128,6144]{1,0:T(8,128)(2,1)}) async-done(((bf16[128,6144]{1,0:T(8,128)(2,1)}, bf16[128,6144]{1,0:T(8,128)(2,1)}, bf16[128,6144]{1,0:T(8,128)(2,1)}), (bf16[128,6144]{1,0:T(8,128)(2,1)}, bf16[128,6144]{1,0:T(8,128)(2,1)}, bf16[128,6144]{1,0:T(8,128)(2,1)})) %all-reduce.4.cloned.1.call-update) | async-done | bytes 4718608 | tf_op jit(solution)/shard_map/psum | solution.py:12
  145.9 1.7 constant_dynamic-update-slice_fusion.3
  148.8 1.3 fusion.23
  150.2 1.1 constant_dynamic-slice_fusion.1
  151.3 134.2 %while.10 = (s32[]{:T(128)}, bf16[3,2,1536,64]{2,3,1,0:T(8,128)(2,1)}, s32[3]{0:T(128)S(1)}, s32[3]{0:T(128)S(1)}, s32[3]{0:T(128)S(1)}, /*index=5*/bf16[2,2,153...) while((s32[]{:T(128)}, ...), condition=%wide.region_6.7_spmd, body=%wide.region_4.6_spmd.sunk | while | flops 393228 | bytes 7078207 | solution.py:62
  159.0 34.9 %all-reduce.6.cloned.1.call-done = bf16[1,2,1536,64]{3,2,1,0:T(8,128)(2,1)} async-done(((bf16[1,2,1536,64]{3,2,1,0:T(8,128)(2,1)}), bf16[1,2,1536,64]{3,2,1,0:T(8,128)(2,1)}) %all-reduce.6.cloned.1.call-update) | async-done | bytes 393232 | tf_op jit(solution)/shard_map/while/body/eval_jaxpr/psum | solution.py:12
  193.9 1.4 copy.36
  203.8 34.8 %all-reduce.6.cloned.1.call-done = bf16[1,2,1536,64]{3,2,1,0:T(8,128)(2,1)} async-done(((bf16[1,2,1536,64]{3,2,1,0:T(8,128)(2,1)}), bf16[1,2,1536,64]{3,2,1,0:T(8,128)(2,1)}) %all-reduce.6.cloned.1.call-update) | async-done | bytes 393232 | tf_op jit(solution)/shard_map/while/body/eval_jaxpr/psum | solution.py:12
  238.6 1.4 copy.36
  248.5 34.8 %all-reduce.6.cloned.1.call-done = bf16[1,2,1536,64]{3,2,1,0:T(8,128)(2,1)} async-done(((bf16[1,2,1536,64]{3,2,1,0:T(8,128)(2,1)}), bf16[1,2,1536,64]{3,2,1,0:T(8,128)(2,1)}) %all-reduce.6.cloned.1.call-update) | async-done | bytes 393232 | tf_op jit(solution)/shard_map/while/body/eval_jaxpr/psum | solution.py:12
  283.3 1.4 copy.36
  285.5 2.2 fusion.24
  287.7 19.7 %all-gather.1 = f32[12,128,2,64]{1,3,2,0:T(8,128)S(1)} all-gather(f32[3,128,2,64]{1,3,2,0:T(8,128)S(1)} %bitcast.72), channel_id=3, replica_groups=mesh['groups'=2,'wide'=4,'expert'=4] {'expert'}, dimensions={0}, use_global_device_ids=true | all-gather | bytes 983040 | tf_op jit(solution)/shard_map/all_gather | solution.py:66
  308.5 1.2 slice-done.1
  309.6 15.1 %fusion.2 = f32[384,2,1024]{2,0,1:T(8,128)} fusion(bf16[2,6144,1024]{2,1,0:T(8,128)(2,1)} %param.19, bf16[384,6144]{1,0:T(8,128)(2,1)S(1)} %bitcast.68), kind=kOutput, calls=%fused_computation.6 | convolution fusion | flops 9663676416 | bytes 33030144 | tf_op jit(solution)/shard_map/td,edf->tef/dot_general | solution.py:79
  324.8 16.2 %fusion.5 = bf16[384,2,1024]{2,0,1:T(8,128)(2,1)} fusion(f32[3,128,2,1024]{3,1,0,2:T(8,128)S(1)} %copy.22, f32[384,2,1024]{2,0,1:T(8,128)} %fusion.2, f32[384,2]{0,1:T(2,128)S(1)} %fusion.17, bf16[2,6144,1024]{2,1,0:T(8,128)(2,1)} %param.20, bf16[384,6144]{1,0:T(8,128)(2,1)S(1)} %bitcast.68), kind=kOutput, calls=%fused_computation.10 | convolution fusion | flops 9669967872 | bytes 37751808 | tf_op jit(solution)/shard_map/td,edf->tef/dot_general | solution.py:83
  341.2 113.7 %all-gather.5.cloned.1.call-done = bf16[384,2,4096]{2,0,1:T(8,128)(2,1)} async-done(((bf16[384,2,1024]{2,0,1:T(8,128)(2,1)}), bf16[384,2,4096]{2,0,1:T(8,128)(2,1)}) %all-gather.5.cloned.1.call-update) | async-done | bytes 6291472 | tf_op jit(solution)/shard_map/all_gather | solution.py:89
  454.9 17.7 %convolution_bitcast_fusion = f32[384,1536]{1,0:T(8,128)} fusion(bf16[384,2,4096]{2,0,1:T(8,128)(2,1)} %all-gather.5.cloned.1.call-done, bf16[2,4096,1536]{2,1,0:T(8,128)(2,1)} %param.21), kind=kOutput, calls=%fused_computation.12 | convolution fusion | flops 9663676416 | bytes 33816576 | tf_op jit(solution)/shard_map/tef,efd->td/dot_general | solution.py:87
  472.6 31.4 %reduce-scatter.2.cloned.1.call-done = f32[96,1536]{1,0:T(8,128)} async-done(((f32[384,1536]{1,0:T(8,128)}), f32[96,1536]{1,0:T(8,128)}) %reduce-scatter.2.cloned.1.call-update) | async-done | bytes 589840 | tf_op jit(solution)/shard_map/reduce_scatter | solution.py:93
  504.0 1.8 convert_element_type.20
  (77 shorter events, 16.4 us)
Async XLA Ops:
  6.5 47.3 %copy-start = (bf16[8,2,64,1024]{3,2,1,0:T(8,128)(2,1)S(1)}, bf16[8,2,64,1024]{3,2,1,0:T(8,128)(2,1)}, u32[]{:S(2)}) copy-start(bf16[8,2,64,1024]{3,2,1,0:T(8,128)(2,1)} %param.23) | copy-start | bytes 6291460
  6.5 42.2 %all-gather.7.cloned.1.call-start = ((), (), s32[]{:S(2)}) async-start(), calls=%async_computation.3 | async-start | bytes 1966080 | tf_op jit(solution)/shard_map/all_gather | solution.py:31
  7.3 138.6 %all-reduce.4.cloned.1.call-start = ((), (), s32[]{:S(2)}) async-start(), calls=%async_computation.4 | async-start | bytes 9437184 | tf_op jit(solution)/shard_map/psum | solution.py:12
  52.4 0.7 copy-start.10
  52.4 0.7 copy-start.2
  52.4 1.3 copy-start.9
  145.9 1.9 copy-start.7
  145.9 2.4 copy-start.6
  147.8 1.0 copy-start.8
  148.8 2.5 copy-start.3
  148.8 2.5 copy-start.4
  151.3 42.6 %all-reduce.6.cloned.1.call-start = ((), (), s32[]{:S(2)}) async-start(), calls=%async_computation.5 | async-start | bytes 1572864 | tf_op jit(solution)/shard_map/while/body/eval_jaxpr/psum | solution.py:12
  196.1 42.5 %all-reduce.6.cloned.1.call-start = ((), (), s32[]{:S(2)}) async-start(), calls=%async_computation.5 | async-start | bytes 1572864 | tf_op jit(solution)/shard_map/while/body/eval_jaxpr/psum | solution.py:12
  240.8 42.5 %all-reduce.6.cloned.1.call-start = ((), (), s32[]{:S(2)}) async-start(), calls=%async_computation.5 | async-start | bytes 1572864 | tf_op jit(solution)/shard_map/while/body/eval_jaxpr/psum | solution.py:12
  285.5 21.9 %copy-start.5 = (bf16[3,2,64,1024]{3,0,2,1:T(4,128)(2,1)S(1)}, bf16[3,2,64,1024]{3,0,2,1:T(4,128)(2,1)}, u32[]{:S(2)}) copy-start(bf16[3,2,64,1024]{3,0,2,1:T(4,128)(2,1)} %fusion.10) | copy-start | bytes 2359300
  285.5 169.4 %all-gather.5.cloned.1.call-start = ((), (), s32[]{:S(2)}) async-start(), calls=%async_computation.1 | async-start | bytes 7864320 | tf_op jit(solution)/shard_map/all_gather | solution.py:89
  285.5 23.0 %slice-start = ((s8[4718592]{0:T(1024)(128)(4,1)}), s8[524288]{0:T(1024)(128)(4,1)S(1)}, s32[]{:S(2)}) async-start(s8[4718592]{0:T(1024)(128)(4,1)} %bitcast.67), calls=%async_computation.6 | async-start | bytes 1048576
  307.4 2.2 slice-start.1
  341.0 163.0 %reduce-scatter.2.cloned.1.call-start = ((), (), s32[]{:S(2)}) async-start(), calls=%async_computation.2 | async-start | bytes 2949120 | tf_op jit(solution)/shard_map/reduce_scatter | solution.py:93
  454.9 50.9 %copy-start.1 = (bf16[8,2,64,1024]{3,2,1,0:T(8,128)(2,1)S(1)}, bf16[8,2,64,1024]{3,2,1,0:T(8,128)(2,1)}, u32[]{:S(2)}) copy-start(bf16[8,2,64,1024]{3,2,1,0:T(8,128)(2,1)} %param.23) | copy-start | bytes 6291460
Sparse Core Ops, SparseCore 0:
  8.9 39.7 all-gather.6
  52.6 93.2 all-reduce.3
  159.2 34.7 all-reduce.5
  203.9 34.6 all-reduce.5
  248.6 34.6 all-reduce.5
  341.1 113.7 all-gather.4
  472.7 31.2 reduce-scatter.1
